TPU v7x, 32 devices: a whole 2x2x4 slice. The times are simulated.
32 devices in a mesh: ctx: 4 (over y, core), ep: 8 (over z, x).
Axes of the slice: x: 2, y: 2, z: 4, core: 2. Of those that a mesh axis runs over, the one named last changes fastest.
Arguments:
- tokens: bfloat16 [1024, 3584], P('ep', 'ctx'), may hold values from -6 to 6
- cotangent: bfloat16 [1024, 3584], P('ep', 'ctx'), may hold values from -0.8984375 to 0.8984375
- expert_ids: int32 [1024, 1], P('ep'), may hold values from 0 to 7; in each aligned block of 128 rows (0 to 127, 128 to 255, ...) at most 24 rows name the same one
- route_gates: float32 [1024, 1], P('ep'), may hold values from 0.1 to 1
- w_gate: bfloat16 [8, 3584, 2048], P('ep', None, 'ctx'), may hold values from -0.125 to 0.125
- w_up: bfloat16 [8, 3584, 2048], P('ep', None, 'ctx'), may hold values from -0.09375 to 0.09375
- w_down: bfloat16 [8, 2048, 3584], P('ep', 'ctx'), may hold values from -0.1875 to 0.1875
Outputs:
- layer_out: bfloat16 [1024, 3584], P('ep', 'ctx')
- input_grad: bfloat16 [1024, 3584], P('ep', 'ctx')
- gate_grad: float32 [1024, 1], P('ep')
- w_gate_grad: bfloat16 [8, 3584, 2048], P('ep', None, 'ctx')
- w_up_grad: bfloat16 [8, 3584, 2048], P('ep', None, 'ctx')
Inputs may be any that keep to these rules, and one draw needn't show every extreme that they name: `expert_ids`: within each aligned block of 128 tokens (the tokens of one index of ep) no expert is named more than 24 times, a bound that some block reaches; the routes of one token name different experts.
All inputs are finite; a program needn't handle non-finite values.
Results may differ from a plain program's by a relative error of at most 0.015.
Values may be sent and summed in bfloat16 or wider, within the bound.
No kernel may reach another device: no remote copies, remote signals or barrier semaphores. Data moves between devices by JAX's collectives and lax.ppermute only.
A program may use at most 128 MiB of HBM per device.

v0:
```python
import jax
import jax.numpy as jnp
from jax import lax
from jax.sharding import PartitionSpec as P


def route_tables(expert_ids, experts, capacity):
    tok_rows, routes = expert_ids.shape
    flat_ids = expert_ids.reshape(-1)
    labels = jnp.arange(experts, dtype=jnp.int32)
    onehot = (flat_ids[:, None] == labels[None, :]).astype(jnp.int32)
    earlier = jnp.cumsum(onehot, axis=0) - onehot
    slot_rank = jnp.sum(earlier * onehot, axis=1)
    slot_ids = (flat_ids * capacity + slot_rank).reshape(tok_rows, routes)
    positions = jnp.arange(experts * capacity, dtype=jnp.int32)
    return [slot_ids[:, 0][:, None] == positions[None, :]]


def shards(tokens, cotangent, expert_ids, route_gates, w_gate, w_up, w_down):
    tok_rows, routes = expert_ids.shape
    experts = lax.axis_size("ep")
    capacity = 3 * tok_rows * routes // (2 * experts)
    slot_count = experts * capacity
    col_width = tokens.shape[1]
    route_maps = route_tables(expert_ids, experts, capacity)
    chosen = route_maps[0].astype(jnp.bfloat16)
    slot_gates = jnp.sum(jnp.where(route_maps[0], route_gates[:, 0][:, None], 0.0), axis=0)
    slot_gates = slot_gates.reshape(experts, capacity)

    def place_rows(values):
        placed = jnp.einsum("ts,tc->sc", chosen, values, preferred_element_type=jnp.float32)
        return placed.astype(jnp.bfloat16).reshape(experts, capacity, values.shape[1])

    sent_inputs = place_rows(tokens)
    sent_grads = place_rows(cotangent)
    got_inputs, got_grads, got_gates = (
        lax.all_to_all(sent_inputs, "ep", split_axis=0, concat_axis=0, tiled=True),
        lax.all_to_all(sent_grads, "ep", split_axis=0, concat_axis=0, tiled=True),
        lax.all_to_all(
            slot_gates.astype(jnp.bfloat16), "ep", split_axis=0, concat_axis=0, tiled=True
        ).astype(slot_gates.dtype),
    )
    slot_inputs, slot_grads = (
        lax.all_gather(got_inputs, "ctx", axis=2, tiled=True),
        lax.all_gather(got_grads, "ctx", axis=2, tiled=True),
    )
    width = slot_inputs.shape[2]
    rows_in = slot_inputs.reshape(slot_count, width)
    grads_in = slot_grads.reshape(slot_count, width)
    gate_column = got_gates.reshape(slot_count, 1)
    gate_w = w_gate[0]
    up_w = w_up[0]
    down_w = w_down[0]
    pre_gate = jnp.dot(rows_in, gate_w, preferred_element_type=jnp.float32)
    pre_up = jnp.dot(rows_in, up_w, preferred_element_type=jnp.float32)
    sigma = jax.nn.sigmoid(pre_gate)
    activated = pre_gate * sigma
    hidden = (activated * pre_up).astype(jnp.bfloat16)
    partial_out = jnp.dot(hidden, down_w, preferred_element_type=jnp.float32).reshape(
        experts, capacity, width
    )
    expert_out = lax.psum_scatter(
        partial_out.astype(jnp.bfloat16), "ctx", scatter_dimension=2, tiled=True
    )
    contract_last = (((1,), (1,)), ((), ()))
    hidden_grad = gate_column * lax.dot_general(
        grads_in, down_w, contract_last, preferred_element_type=jnp.float32
    )
    grad_gate = (hidden_grad * pre_up * sigma * (1.0 + pre_gate * (1.0 - sigma))).astype(
        jnp.bfloat16
    )
    grad_up = (hidden_grad * activated).astype(jnp.bfloat16)
    contract_first = (((0,), (0,)), ((), ()))
    w_gate_grad = lax.dot_general(
        rows_in, grad_gate, contract_first, preferred_element_type=jnp.float32
    ).astype(jnp.bfloat16)[None]
    w_up_grad = lax.dot_general(
        rows_in, grad_up, contract_first, preferred_element_type=jnp.float32
    ).astype(jnp.bfloat16)[None]
    back_out = lax.all_to_all(expert_out, "ep", split_axis=0, concat_axis=0, tiled=True)
    back_terms = lax.dot_general(
        grad_gate, gate_w, contract_last, preferred_element_type=jnp.float32
    )
    back_terms = back_terms + lax.dot_general(
        grad_up, up_w, contract_last, preferred_element_type=jnp.float32
    )
    summed = lax.psum_scatter(
        back_terms.reshape(experts, capacity, width).astype(jnp.bfloat16),
        "ctx",
        scatter_dimension=2,
        tiled=True,
    )
    back_grad = lax.all_to_all(summed, "ep", split_axis=0, concat_axis=0, tiled=True)
    out_rows = back_out.reshape(slot_count, col_width)
    grad_rows = back_grad.reshape(slot_count, col_width)
    cotangent_wide = cotangent.astype(jnp.float32)
    route_matrix = route_maps[0].astype(jnp.bfloat16)
    picked = jnp.dot(route_matrix, out_rows, preferred_element_type=jnp.float32)
    layer_out = route_gates[:, 0][:, None] * picked
    gate_terms = [jnp.sum(picked * cotangent_wide, axis=1)]
    input_grad = jnp.dot(route_matrix, grad_rows, preferred_element_type=jnp.float32)
    gate_grad = lax.psum(jnp.stack(gate_terms, axis=1), "ctx")
    return (
        layer_out.astype(jnp.bfloat16),
        input_grad.astype(jnp.bfloat16),
        gate_grad,
        w_gate_grad,
        w_up_grad,
    )


def solution(mesh):
    in_specs = (
        P("ep", "ctx"),
        P("ep", "ctx"),
        P("ep", None),
        P("ep", None),
        P("ep", None, "ctx"),
        P("ep", None, "ctx"),
        P("ep", "ctx", None),
    )
    out_specs = (
        P("ep", "ctx"),
        P("ep", "ctx"),
        P("ep", None),
        P("ep", None, "ctx"),
        P("ep", None, "ctx"),
    )
    return jax.shard_map(shards, mesh=mesh, in_specs=in_specs, out_specs=out_specs, check_vma=False)
```

profile of v0, /device:TPU:0, one launch (start us, length us, event | category | flops | bytes accessed | tf_op | source)
XLA Modules:
  0.0 184.7 jit_solution(12868758092519926794)
XLA Ops:
  7.2 0.8 fusion.18
  8.2 0.8 select_reduce_fusion.1
  9.0 0.7 fusion.23
  10.0 18.3 %all_to_all.26 = bf16[8,24,896]{2,1,0:T(8,128)(2,1)} all-to-all(bf16[8,24,896]{2,1,0:T(8,128)(2,1)S(1)} %bitcast.69), channel_id=1, replica_groups=mesh['ctx'=4,'ep'=8] {'ep'}, dimensions={0} | all-to-all | bytes 688128 | tf_op jit(solution)/shard_map/all_to_all | solution.py:37
  28.4 1.2 convolution_convert_fusion.3
  29.6 14.0 %all_to_all.27 = bf16[8,24,896]{2,1,0:T(8,128)(2,1)} all-to-all(bf16[8,24,896]{2,1,0:T(8,128)(2,1)S(1)} %bitcast.70), channel_id=1, replica_groups=mesh['ctx'=4,'ep'=8] {'ep'}, dimensions={0} | all-to-all | bytes 688128 | tf_op jit(solution)/shard_map/all_to_all | solution.py:38
  43.9 9.3 %all_to_all.28 = bf16[8,1,24]{2,1,0:T(2,128)(2,1)S(1)} all-to-all(bf16[8,1,24]{2,1,0:T(2,128)(2,1)S(1)} %convert_element_type.86), channel_id=1, replica_groups=mesh['ctx'=4,'ep'=8] {'ep'}, dimensions={0} | all-to-all | bytes 768 | tf_op jit(solution)/shard_map/all_to_all | solution.py:39
  53.3 3.8 %fusion.11 = f32[192,512]{1,0:T(8,128)S(1)} fusion(bf16[192,3584]{1,0:T(8,128)(2,1)} %bitcast.63, bf16[1,3584,512]{2,1,0:T(8,128)(2,1)} %param.11), kind=kOutput, calls=%fused_computation.15 | convolution fusion | flops 704643072 | bytes 5439488 | tf_op jit(solution)/shard_map/dot_general | solution.py:54
  57.6 0.9 fusion.7
  58.4 7.3 %all-gather.5.cloned.1.call-done = bf16[8,24,3584]{2,1,0:T(8,128)(2,1)} async-done(((bf16[8,24,896]{2,1,0:T(8,128)(2,1)}), bf16[8,24,3584]{2,1,0:T(8,128)(2,1)}) %all-gather.5.cloned.1.call-update) | async-done | bytes 1376272 | tf_op jit(solution)/shard_map/all_gather | solution.py:45
  65.7 4.0 %multiply_convert_fusion.1 = (bf16[192,512]{1,0:T(8,128)(2,1)S(1)}, bf16[192,512]{1,0:T(8,128)(2,1)S(1)}, bf16[192,512]{1,0:T(8,128)(2,1)S(1)}) fusion(f32[192,512]{1,0:T(8,128)S(1)} %fusion.11, f32[192,512]{1,0:T(8,128)S(1)} %fusion.7, bf16[192,3584]{1,0:T(8,128)(2,1)} %bitcast.77, bf16[1,512,3584]{2,1,0:T(8,128)(2,1)} %param.13, f32[192]{0:T(256)S(1)} %reshape.62), kind=kOutput, calls=%fused_computation.23 | convolution fusion | flops 706215936 | bytes 6423296 | tf_op jit(solution)/shard_map/dot_general | solution.py:66
  69.8 0.9 convolution_convert_fusion.2
  70.7 6.4 %copy.14 = bf16[8,24,3584]{1,0,2:T(8,128)(2,1)} copy(bf16[8,24,3584]{2,1,0:T(8,128)(2,1)S(1)} %convolution_convert_fusion.2) | data formatting | bytes 2752512
  77.1 9.6 %reshape.64 = bf16[3584,192]{1,0:T(8,128)(2,1)} reshape(bf16[3584,8,24]{2,1,0:T(8,128)(2,1)} %bitcast.59) | data formatting | bytes 2752512
  86.8 3.5 %fusion.9 = f32[192,3584]{1,0:T(8,128)S(1)} fusion(bf16[192,512]{1,0:T(8,128)(2,1)S(1)} %get-tuple-element.6, bf16[1,3584,512]{2,1,0:T(8,128)(2,1)} %param.11), kind=kOutput, calls=%fused_computation.13 | convolution fusion | flops 704643072 | bytes 6619136 | tf_op jit(solution)/shard_map/dot_general | solution.py:81
  90.4 1.3 fusion.2
  91.7 6.4 %copy.16 = bf16[8,24,3584]{1,0,2:T(8,128)(2,1)} copy(bf16[8,24,3584]{2,1,0:T(8,128)(2,1)S(1)} %bitcast.67) | data formatting | bytes 2752512
  98.1 9.6 %reshape.66 = bf16[3584,192]{1,0:T(8,128)(2,1)} reshape(bf16[3584,8,24]{2,1,0:T(8,128)(2,1)} %bitcast.60) | data formatting | bytes 2752512
  107.7 9.0 %reduce-scatter.7.cloned.1.call-done = bf16[896,192]{1,0:T(8,128)(2,1)} async-done(((bf16[3584,192]{1,0:T(8,128)(2,1)}), bf16[896,192]{1,0:T(8,128)(2,1)}) %reduce-scatter.7.cloned.1.call-update) | async-done | bytes 344080
  116.7 2.6 %reshape.65 = bf16[896,8,24]{2,1,0:T(8,128)(2,1)S(1)} reshape(bf16[896,192]{1,0:T(8,128)(2,1)} %reduce-scatter.7.cloned.1.call-done) | data formatting | bytes 688128
  119.3 2.4 %copy.15 = bf16[8,24,896]{2,1,0:T(8,128)(2,1)} copy(bf16[8,24,896]{1,0,2:T(8,128)(2,1)S(1)} %bitcast.61) | data formatting | bytes 688128
  121.6 5.5 %all-to-all-start.1 = ((bf16[8,24,896]{2,1,0:T(8,128)(2,1)}), bf16[8,24,896]{2,1,0:T(8,128)(2,1)}, u32[]{:S(2)}, u32[]{:S(2)}) async-start(bf16[8,24,896]{2,1,0:T(8,128)(2,1)} %copy.15), calls=%async_computation.1 | async-start | bytes 688128 | tf_op jit(solution)/shard_map/all_to_all | solution.py:80
  127.1 22.6 %reduce-scatter.9.cloned.1.call-done = bf16[896,192]{1,0:T(8,128)(2,1)} async-done(((bf16[3584,192]{1,0:T(8,128)(2,1)}), bf16[896,192]{1,0:T(8,128)(2,1)}) %reduce-scatter.9.cloned.1.call-update) | async-done | bytes 344080
  149.7 2.6 %reshape.67 = bf16[896,8,24]{2,1,0:T(8,128)(2,1)S(1)} reshape(bf16[896,192]{1,0:T(8,128)(2,1)} %reduce-scatter.9.cloned.1.call-done) | data formatting | bytes 688128
  152.2 2.4 %copy.17 = bf16[8,24,896]{2,1,0:T(8,128)(2,1)} copy(bf16[8,24,896]{1,0,2:T(8,128)(2,1)S(1)} %bitcast.62) | data formatting | bytes 688128
  154.6 5.5 %all-to-all-start.4 = ((bf16[8,24,896]{2,1,0:T(8,128)(2,1)}), bf16[8,24,896]{2,1,0:T(8,128)(2,1)S(1)}, u32[]{:S(2)}, u32[]{:S(2)}) async-start(bf16[8,24,896]{2,1,0:T(8,128)(2,1)} %copy.17), calls=%async_computation.4 | async-start | bytes 688128 | tf_op jit(solution)/shard_map/all_to_all | solution.py:93
  160.1 4.0 %fusion = bf16[1,3584,512]{2,1,0:T(8,128)(2,1)} fusion(bf16[192,3584]{1,0:T(8,128)(2,1)S(1)} %bitcast.65, bf16[192,512]{1,0:T(8,128)(2,1)} %copy-done.6), kind=kOutput, calls=%fused_computation.2 | convolution fusion | flops 706478080 | bytes 5242880 | tf_op jit(solution)/shard_map/dot_general | solution.py:74
  164.1 3.0 %fusion.1 = bf16[1,3584,512]{2,1,0:T(8,128)(2,1)} fusion(bf16[192,3584]{1,0:T(8,128)(2,1)S(1)} %bitcast.66, bf16[192,512]{1,0:T(8,128)(2,1)S(1)} %copy-done.8), kind=kOutput, calls=%fused_computation.3 | convolution fusion | flops 706478080 | bytes 5242880 | tf_op jit(solution)/shard_map/dot_general | solution.py:77
  167.1 2.0 %multiply_reduce_fusion = (f32[128]{0:T(128)S(1)}, bf16[128,896]{1,0:T(8,128)(2,1)}) fusion(bf16[128,896]{1,0:T(8,128)(2,1)S(1)} %copy-done.5, f32[128]{0:T(128)S(1)} %bitcast.75, bf16[192,896]{1,0:T(8,128)(2,1)} %bitcast.11, s32[128]{0:T(128)S(1)} %fusion.23), kind=kOutput, calls=%fused_computation.21 | convolution fusion | flops 44638080 | bytes 804352 | tf_op jit(solution)/shard_map/dot_general | solution.py:98
  169.1 1.6 all-to-all-done.4
  170.8 1.0 convolution_convert_fusion.5
  171.7 6.4 %psum.7 = f32[128,1]{0,1:T(1,128)} all-reduce(f32[128,1]{0,1:T(1,128)S(1)} %bitcast.76), channel_id=1, replica_groups=mesh['ctx'=4,'ep'=8] {'ctx'}, use_global_device_ids=true, to_apply=%region_6.7 | all-reduce | flops 128 | bytes 1024 | tf_op jit(solution)/shard_map/psum | solution.py:102
  (36 shorter events, 1.5 us)
Async XLA Ops:
  7.2 2.5 %copy-start = (bf16[128,896]{1,0:T(8,128)(2,1)S(1)}, bf16[128,896]{1,0:T(8,128)(2,1)}, u32[]{:S(2)}) copy-start(bf16[128,896]{1,0:T(8,128)(2,1)} %param.7) | copy-start | bytes 688132
  7.2 36.5 %copy-start.9 = (f32[128,1]{0,1:T(1,128)S(1)}, f32[128,1]{0,1:T(1,128)}, u32[]{:S(2)}) copy-start(f32[128,1]{0,1:T(1,128)} %param.10) | copy-start | bytes 1540
  7.2 46.1 %all-gather.3.cloned.1.call-start = ((), (), s32[]{:S(2)}) async-start(), calls=%async_computation.7 | async-start | bytes 1720320 | tf_op jit(solution)/shard_map/all_gather | solution.py:44
  28.3 37.4 %all-gather.5.cloned.1.call-start = ((), (), s32[]{:S(2)}) async-start(), calls=%async_computation.8 | async-start | bytes 1720320 | tf_op jit(solution)/shard_map/all_gather | solution.py:45
  43.7 73.0 %reduce-scatter.7.cloned.1.call-start = ((), (), s32[]{:S(2)}) async-start(), calls=%async_computation.9 | async-start | bytes 2293760
  53.3 3.9 %copy-start.1 = (bf16[1,3584,512]{2,1,0:T(8,128)(2,1)S(1)}, bf16[1,3584,512]{2,1,0:T(8,128)(2,1)}, u32[]{:S(2)}) copy-start(bf16[1,3584,512]{2,1,0:T(8,128)(2,1)} %param.12) | copy-start | bytes 11010052
  53.3 4.3 %copy-start.3 = (bf16[8,24,3584]{2,1,0:T(8,128)(2,1)S(1)}, bf16[8,24,3584]{2,1,0:T(8,128)(2,1)}, u32[]{:S(2)}) copy-start(bf16[8,24,3584]{2,1,0:T(8,128)(2,1)} %all-gather.3.cloned.1.call-done) | copy-start | bytes 4128772
  65.7 4.1 %copy-start.4 = (bf16[1,512,3584]{2,1,0:T(8,128)(2,1)S(1)}, bf16[1,512,3584]{2,1,0:T(8,128)(2,1)}, u32[]{:S(2)}) copy-start(bf16[1,512,3584]{2,1,0:T(8,128)(2,1)} %param.13) | copy-start | bytes 11010052
  69.8 17.0 %copy-start.6 = (bf16[192,512]{1,0:T(8,128)(2,1)}, bf16[192,512]{1,0:T(8,128)(2,1)S(1)}, u32[]{:S(2)}) copy-start(bf16[192,512]{1,0:T(8,128)(2,1)S(1)} %get-tuple-element.6) | copy-start | bytes 589828
  69.8 20.6 %copy-start.7 = (bf16[192,512]{1,0:T(8,128)(2,1)}, bf16[192,512]{1,0:T(8,128)(2,1)S(1)}, u32[]{:S(2)}) copy-start(bf16[192,512]{1,0:T(8,128)(2,1)S(1)} %get-tuple-element.5) | copy-start | bytes 589828
  86.7 62.9 %reduce-scatter.9.cloned.1.call-start = ((), (), s32[]{:S(2)}) async-start(), calls=%async_computation.10 | async-start | bytes 2293760
  86.8 3.6 %copy-start.2 = (bf16[1,3584,512]{2,1,0:T(8,128)(2,1)S(1)}, bf16[1,3584,512]{2,1,0:T(8,128)(2,1)}, u32[]{:S(2)}) copy-start(bf16[1,3584,512]{2,1,0:T(8,128)(2,1)} %param.12) | copy-start | bytes 11010052
  121.6 33.0 %all-to-all-start.1 = ((bf16[8,24,896]{2,1,0:T(8,128)(2,1)}), bf16[8,24,896]{2,1,0:T(8,128)(2,1)}, u32[]{:S(2)}, u32[]{:S(2)}) async-start(bf16[8,24,896]{2,1,0:T(8,128)(2,1)} %copy.15), calls=%async_computation.1 | async-start | bytes 688128 | tf_op jit(solution)/shard_map/all_to_all | solution.py:80
  154.6 16.2 %all-to-all-start.4 = ((bf16[8,24,896]{2,1,0:T(8,128)(2,1)}), bf16[8,24,896]{2,1,0:T(8,128)(2,1)S(1)}, u32[]{:S(2)}, u32[]{:S(2)}) async-start(bf16[8,24,896]{2,1,0:T(8,128)(2,1)} %copy.17), calls=%async_computation.4 | async-start | bytes 688128 | tf_op jit(solution)/shard_map/all_to_all | solution.py:93
  160.1 4.0 %copy-start.8 = (bf16[192,512]{1,0:T(8,128)(2,1)S(1)}, bf16[192,512]{1,0:T(8,128)(2,1)}, u32[]{:S(2)}) copy-start(bf16[192,512]{1,0:T(8,128)(2,1)} %copy-done.7) | copy-start | bytes 589828
  164.1 3.0 %copy-start.5 = (bf16[128,896]{1,0:T(8,128)(2,1)S(1)}, bf16[128,896]{1,0:T(8,128)(2,1)}, u32[]{:S(2)}) copy-start(bf16[128,896]{1,0:T(8,128)(2,1)} %param.8) | copy-start | bytes 688132
Sparse Core Ops, SparseCore 0:
  28.5 17.0 all-gather.2
  47.1 18.5 all-gather.4
  86.8 29.7 reduce-scatter.6
  119.8 29.8 reduce-scatter.8
where the time goes:
time: 186 us; the launch traced here: 185 us
  blocking collectives  48.1 us (26%)
  local copies, waits for them, and re-layouts  42.5 us (23%)
  waiting for transfers between devices  40.5 us (22%)
  matrix products  25.9 us (14%)
  between operations  13.9 us (7%)
  starting transfers between devices  11.2 us (6%)
  other arithmetic  2.59 us (1%)
    unnamed x28, local copies, waits for them, and re-layouts  42.3 us
    unnamed x6, waiting for transfers between devices  31.6 us
    all_to_all x1, blocking collectives, shards(): lax.all_to_all(sent_inputs, 'ep', split_axis=0, concat_axis=0, tiled=True)  18.3 us
    all_to_all x1, blocking collectives, shards(): lax.all_to_all(sent_grads, 'ep', split_axis=0, concat_axis=0, tiled=True)  14 us
    all_to_all x1, blocking collectives, shards(): lax.all_to_all(slot_gates.astype(jnp.bfloat16), 'ep', split_axis=0, conca...  9.28 us
    all_gather x1, waiting for transfers between devices, shards(): lax.all_gather(got_grads, 'ctx', axis=2, tiled=True)  7.28 us
    psum x1, blocking collectives, shards(): gate_grad = lax.psum(jnp.stack(gate_terms, axis=1), 'ctx')  6.42 us
    all_to_all x1, starting transfers between devices, shards(): lax.all_to_all(expert_out, 'ep', split_axis=0, concat_axis=0, tiled=True)  5.51 us
  transfers between devices with their start and end apart: 6, of which 4 were waited for; matrix products, arithmetic and copies ran while one was open for 25% of the time, Pallas kernels for 0%

commit v1 on v0

--- a/solution.py
+++ b/solution.py
@@ -2,6 +2,22 @@
 import jax.numpy as jnp
 from jax import lax
 from jax.sharding import PartitionSpec as P
+
+
+def swapped_with_each(shard, axis, split, join):
+    ways, here = (lax.axis_size(axis), lax.axis_index(axis))
+    width = shard.shape[split] // ways
+    shape = list(shard.shape)
+    shape[split] = width
+    height = shape[join]
+    shape[join] = height * ways
+    full = jnp.zeros(shape, shard.dtype)
+    for mask in range(ways):
+        part = lax.dynamic_slice_in_dim(shard, (here ^ mask) * width, width, axis=split)
+        if mask:
+            part = lax.ppermute(part, axis, [(d, d ^ mask) for d in range(ways)])
+        full = lax.dynamic_update_slice_in_dim(full, part, (here ^ mask) * height, axis=join)
+    return full
 
 
 def route_tables(expert_ids, experts, capacity):
@@ -77,7 +93,7 @@
     w_up_grad = lax.dot_general(
         rows_in, grad_up, contract_first, preferred_element_type=jnp.float32
     ).astype(jnp.bfloat16)[None]
-    back_out = lax.all_to_all(expert_out, "ep", split_axis=0, concat_axis=0, tiled=True)
+    back_out = swapped_with_each(expert_out, "ep", 0, 0)
     back_terms = lax.dot_general(
         grad_gate, gate_w, contract_last, preferred_element_type=jnp.float32
     )

time: 186 us -> 188 us (1.011)
  waiting for transfers between devices: 40.5 us -> 21.9 us
  local copies, waits for them, and re-layouts: 42.5 us -> 57.9 us
  starting transfers between devices: 11.2 us -> 18.6 us
  matrix products: 25.9 us -> 23.9 us
    unnamed x6, waiting for transfers between devices: 31.6 us -> 10 us
    ppermute x0 -> x7, starting transfers between devices: none -> 12.7 us  [swapped_with_each(): part = lax.ppermute(part, axis, [(d, d ^ mask) for d in range(ways)])]
    unnamed x28 -> x29, local copies, waits for them, and re-layouts: 42.3 us -> 50.5 us
    all_to_all x1 -> x0, starting transfers between devices: 5.51 us -> none  [shards(): lax.all_to_all(expert_out, 'ep', split_axis=0, concat_axis=0, tiled=True)]
    dynamic_slice x0 -> x1, local copies, waits for them, and re-layouts: none -> 4.75 us  [swapped_with_each(): lax.dynamic_slice_in_dim(shard, (here ^ mask) * width, width, axis=split)]
    ppermute x0 -> x7, waiting for transfers between devices: none -> 4.57 us  [swapped_with_each(): part = lax.ppermute(part, axis, [(d, d ^ mask) for d in range(ways)])]
    dynamic_update_slice x0 -> x8, local copies, waits for them, and re-layouts: none -> 2.46 us  [swapped_with_each(): lax.dynamic_update_slice_in_dim(full, part, (here ^ mask) * height, axis=...]
  transfers between devices with their start and end apart: 6 -> 12, of which waited for: 4 -> 5; matrix products, arithmetic and copies ran while one was open for 25% -> 32% of each run, Pallas kernels for 0% -> 0%
where the time goes in v1:
time: 188 us; the launch traced here: 187 us
  local copies, waits for them, and re-layouts  57.9 us (31%)
  blocking collectives  48.1 us (26%)
  matrix products  23.9 us (13%)
  waiting for transfers between devices  21.9 us (12%)
  starting transfers between devices  18.6 us (10%)
  between operations  14 us (7%)
  other arithmetic  2.59 us (1%)
    unnamed x29, local copies, waits for them, and re-layouts  50.5 us
    all_to_all x1, blocking collectives, shards(): lax.all_to_all(sent_inputs, 'ep', split_axis=0, concat_axis=0, tiled=True)  18.4 us
    all_to_all x1, blocking collectives, shards(): lax.all_to_all(sent_grads, 'ep', split_axis=0, concat_axis=0, tiled=True)  14 us
    ppermute x7, starting transfers between devices, swapped_with_each(): part = lax.ppermute(part, axis, [(d, d ^ mask) for d in range(ways)])  12.7 us
    unnamed x6, waiting for transfers between devices  10 us
    all_to_all x1, blocking collectives, shards(): lax.all_to_all(slot_gates.astype(jnp.bfloat16), 'ep', split_axis=0, conca...  9.28 us
    all_gather x1, waiting for transfers between devices, shards(): lax.all_gather(got_grads, 'ctx', axis=2, tiled=True)  7.29 us
    psum x1, blocking collectives, shards(): gate_grad = lax.psum(jnp.stack(gate_terms, axis=1), 'ctx')  6.4 us
  transfers between devices with their start and end apart: 12, of which 5 were waited for; matrix products, arithmetic and copies ran while one was open for 32% of the time, Pallas kernels for 0%

profile of v1, /device:TPU:0, one launch (start us, length us, event | category | flops | bytes accessed | tf_op | source)
XLA Modules:
  0.0 186.9 jit_solution(9131441421881764725)
XLA Ops:
  10.0 18.4 %all_to_all.21 = bf16[8,24,896]{2,1,0:T(8,128)(2,1)} all-to-all(bf16[8,24,896]{2,1,0:T(8,128)(2,1)S(1)} %bitcast.70), channel_id=1, replica_groups=mesh['ctx'=4,'ep'=8] {'ep'}, dimensions={0} | all-to-all | bytes 688128 | tf_op jit(solution)/shard_map/all_to_all | solution.py:53
  29.6 14.0 %all_to_all.22 = bf16[8,24,896]{2,1,0:T(8,128)(2,1)} all-to-all(bf16[8,24,896]{2,1,0:T(8,128)(2,1)S(1)} %bitcast.71), channel_id=1, replica_groups=mesh['ctx'=4,'ep'=8] {'ep'}, dimensions={0} | all-to-all | bytes 688128 | tf_op jit(solution)/shard_map/all_to_all | solution.py:54
  43.9 9.3 %all_to_all.23 = bf16[8,1,24]{2,1,0:T(2,128)(2,1)S(1)} all-to-all(bf16[8,1,24]{2,1,0:T(2,128)(2,1)S(1)} %convert_element_type.86), channel_id=1, replica_groups=mesh['ctx'=4,'ep'=8] {'ep'}, dimensions={0} | all-to-all | bytes 768 | tf_op jit(solution)/shard_map/all_to_all | solution.py:55
  53.3 3.8 %fusion.11 = f32[192,512]{1,0:T(8,128)S(1)} fusion(bf16[192,3584]{1,0:T(8,128)(2,1)} %bitcast.63, bf16[1,3584,512]{2,1,0:T(8,128)(2,1)} %param.11), kind=kOutput, calls=%fused_computation.15 | convolution fusion | flops 704643072 | bytes 5439488 | tf_op jit(solution)/shard_map/dot_general | solution.py:70
  58.4 7.3 %all-gather.5.cloned.1.call-done = bf16[8,24,3584]{2,1,0:T(8,128)(2,1)} async-done(((bf16[8,24,896]{2,1,0:T(8,128)(2,1)}), bf16[8,24,3584]{2,1,0:T(8,128)(2,1)}) %all-gather.5.cloned.1.call-update) | async-done | bytes 1376272 | tf_op jit(solution)/shard_map/all_gather | solution.py:61
  65.7 4.0 %multiply_convert_fusion.1 = (bf16[192,512]{1,0:T(8,128)(2,1)S(1)}, bf16[192,512]{1,0:T(8,128)(2,1)S(1)}, bf16[192,512]{1,0:T(8,128)(2,1)S(1)}) fusion(f32[192,512]{1,0:T(8,128)S(1)} %fusion.11, f32[192,512]{1,0:T(8,128)S(1)} %fusion.7, bf16[192,3584]{1,0:T(8,128)(2,1)} %bitcast.78, bf16[1,512,3584]{2,1,0:T(8,128)(2,1)} %param.13, f32[192]{0:T(256)S(1)} %reshape.62), kind=kOutput, calls=%fused_computation.23 | convolution fusion | flops 706215936 | bytes 6423296 | tf_op jit(solution)/shard_map/dot_general | solution.py:82
  70.7 6.3 %copy.14 = bf16[8,24,3584]{1,0,2:T(8,128)(2,1)} copy(bf16[8,24,3584]{2,1,0:T(8,128)(2,1)S(1)} %convolution_convert_fusion.2) | data formatting | bytes 2752512
  77.0 9.6 %reshape.64 = bf16[3584,192]{1,0:T(8,128)(2,1)} reshape(bf16[3584,8,24]{2,1,0:T(8,128)(2,1)} %bitcast.59) | data formatting | bytes 2752512
  86.9 3.5 %fusion.9 = f32[192,3584]{1,0:T(8,128)S(1)} fusion(bf16[192,512]{1,0:T(8,128)(2,1)S(1)} %get-tuple-element.14, bf16[1,3584,512]{2,1,0:T(8,128)(2,1)} %param.11), kind=kOutput, calls=%fused_computation.13 | convolution fusion | flops 704643072 | bytes 6619136 | tf_op jit(solution)/shard_map/dot_general | solution.py:97
  91.8 6.3 %copy.16 = bf16[8,24,3584]{1,0,2:T(8,128)(2,1)} copy(bf16[8,24,3584]{2,1,0:T(8,128)(2,1)S(1)} %bitcast.67) | data formatting | bytes 2752512
  98.1 9.6 %reshape.66 = bf16[3584,192]{1,0:T(8,128)(2,1)} reshape(bf16[3584,8,24]{2,1,0:T(8,128)(2,1)} %bitcast.60) | data formatting | bytes 2752512
  107.8 3.0 %fusion = bf16[1,3584,512]{2,1,0:T(8,128)(2,1)} fusion(bf16[192,3584]{1,0:T(8,128)(2,1)S(1)} %bitcast.65, bf16[192,512]{1,0:T(8,128)(2,1)S(1)} %get-tuple-element.14), kind=kOutput, calls=%fused_computation.2 | convolution fusion | flops 706478080 | bytes 5242880 | tf_op jit(solution)/shard_map/dot_general | solution.py:90
  110.8 3.0 %fusion.1 = bf16[1,3584,512]{2,1,0:T(8,128)(2,1)} fusion(bf16[192,3584]{1,0:T(8,128)(2,1)S(1)} %bitcast.66, bf16[192,512]{1,0:T(8,128)(2,1)S(1)} %get-tuple-element.13), kind=kOutput, calls=%fused_computation.3 | convolution fusion | flops 706478080 | bytes 5242880 | tf_op jit(solution)/shard_map/dot_general | solution.py:93
  113.8 2.8 %reduce-scatter.7.cloned.1.call-done = bf16[896,192]{1,0:T(8,128)(2,1)} async-done(((bf16[3584,192]{1,0:T(8,128)(2,1)}), bf16[896,192]{1,0:T(8,128)(2,1)}) %reduce-scatter.7.cloned.1.call-update) | async-done | bytes 344080
  116.6 2.6 %reshape.65 = bf16[896,8,24]{2,1,0:T(8,128)(2,1)S(1)} reshape(bf16[896,192]{1,0:T(8,128)(2,1)} %reduce-scatter.7.cloned.1.call-done) | data formatting | bytes 688128
  119.2 4.8 %constant_dynamic-slice_fusion = (bf16[1,24,896]{1,0,2:T(2,128)(2,1)S(1)}, bf16[1,24,896]{1,0,2:T(2,128)(2,1)S(1)}, bf16[1,24,896]{1,0,2:T(2,128)(2,1)S(1)}, bf1...) fusion(bf16[8,24,896]{1,0,2:T(8,128)(2,1)S(1)} %bitcast.61, ...), kind=kLoop, calls=%fused_computation.39 | loop fusion | bytes 688160 | tf_op jit(solution)/shard_map/dynamic_slice | solution.py:16
  125.2 1.8 copy.19
  126.9 1.5 collective-permute-start
  128.4 1.8 copy.20
  130.2 1.5 collective-permute-start.1
  131.7 1.8 copy.21
  134.0 1.8 copy.22
  135.7 2.4 %collective-permute-start.3 = (bf16[1,24,896]{2,1,0:T(8,128)(2,1)}, bf16[1,24,896]{2,1,0:T(8,128)(2,1)S(1)}, u32[]{:S(2)}, u32[]{:S(2)}) collective-permute-start(bf16[1,24,896]{2,1,0:T(8,128)(2,1)} %copy.22), channel_id=1, source_target_pairs={{0,4},{1,5},{2,6},{3,7},{4,0},{5,1},{6,2},{7,3},{8,12},{9,13},{10,... | collective-permute-start | bytes 129032 | tf_op jit(solution)/shard_map/ppermute | solution.py:18
  139.3 1.4 collective-permute-start.4
  141.9 7.1 %reduce-scatter.9.cloned.1.call-done = bf16[896,192]{1,0:T(8,128)(2,1)} async-done(((bf16[3584,192]{1,0:T(8,128)(2,1)}), bf16[896,192]{1,0:T(8,128)(2,1)}) %reduce-scatter.9.cloned.1.call-update) | async-done | bytes 344080
  149.0 2.6 %reshape.67 = bf16[896,8,24]{2,1,0:T(8,128)(2,1)S(1)} reshape(bf16[896,192]{1,0:T(8,128)(2,1)} %reduce-scatter.9.cloned.1.call-done) | data formatting | bytes 688128
  151.6 2.4 %copy.17 = bf16[8,24,896]{2,1,0:T(8,128)(2,1)} copy(bf16[8,24,896]{1,0,2:T(8,128)(2,1)S(1)} %bitcast.62) | data formatting | bytes 688128
  154.0 5.5 %all-to-all-start.3 = ((bf16[8,24,896]{2,1,0:T(8,128)(2,1)}), bf16[8,24,896]{2,1,0:T(8,128)(2,1)S(1)}, u32[]{:S(2)}, u32[]{:S(2)}) async-start(bf16[8,24,896]{2,1,0:T(8,128)(2,1)} %copy.17), calls=%async_computation.3 | async-start | bytes 688128 | tf_op jit(solution)/shard_map/all_to_all | solution.py:109
  159.5 3.9 %collective-permute-start.5 = (bf16[1,24,896]{2,1,0:T(8,128)(2,1)S(1)}, bf16[1,24,896]{2,1,0:T(8,128)(2,1)S(1)}, u32[]{:S(2)}, u32[]{:S(2)}) collective-permute-start(bf16[1,24,896]{2,1,0:T(8,128)(2,1)S(1)} %copy.24), channel_id=1, source_target_pairs={{0,6},{1,7},{2,4},{3,5},{4,2},{5,3},{6,0},{7,1},{8,14},{9,15},{10,... | collective-permute-start | bytes 129032 | tf_op jit(solution)/shard_map/ppermute | solution.py:18
  164.2 1.5 collective-permute-start.6
  167.4 3.2 %collective-permute-done.5 = bf16[1,24,896]{2,1,0:T(8,128)(2,1)S(1)} collective-permute-done((bf16[1,24,896]{2,1,0:T(8,128)(2,1)S(1)}, bf16[1,24,896]{2,1,0:T(8,128)(2,1)S(1)}, u32[]{:S(2)}, u32[]{:S(2)}) %collective-permute-start.5) | collective-permute-done | bytes 43040 | tf_op jit(solution)/shard_map/ppermute | solution.py:18
  173.0 6.4 %psum.7 = f32[128,1]{0,1:T(1,128)} all-reduce(f32[128,1]{0,1:T(1,128)S(1)} %bitcast.77), channel_id=1, replica_groups=mesh['ctx'=4,'ep'=8] {'ctx'}, use_global_device_ids=true, to_apply=%region_6.7 | all-reduce | flops 128 | bytes 1024 | tf_op jit(solution)/shard_map/psum | solution.py:118
  (59 shorter events, 18.2 us)
Async XLA Ops:
  7.2 2.5 %copy-start = (bf16[128,896]{1,0:T(8,128)(2,1)S(1)}, bf16[128,896]{1,0:T(8,128)(2,1)}, u32[]{:S(2)}) copy-start(bf16[128,896]{1,0:T(8,128)(2,1)} %param.7) | copy-start | bytes 688132
  7.2 36.5 %copy-start.6 = (f32[128,1]{0,1:T(1,128)S(1)}, f32[128,1]{0,1:T(1,128)}, u32[]{:S(2)}) copy-start(f32[128,1]{0,1:T(1,128)} %param.10) | copy-start | bytes 1540
  7.2 46.1 %all-gather.3.cloned.1.call-start = ((), (), s32[]{:S(2)}) async-start(), calls=%async_computation.6 | async-start | bytes 1720320 | tf_op jit(solution)/shard_map/all_gather | solution.py:60
  28.3 37.4 %all-gather.5.cloned.1.call-start = ((), (), s32[]{:S(2)}) async-start(), calls=%async_computation.7 | async-start | bytes 1720320 | tf_op jit(solution)/shard_map/all_gather | solution.py:61
  43.7 73.0 %reduce-scatter.7.cloned.1.call-start = ((), (), s32[]{:S(2)}) async-start(), calls=%async_computation.8 | async-start | bytes 2293760
  53.3 3.9 %copy-start.1 = (bf16[1,3584,512]{2,1,0:T(8,128)(2,1)S(1)}, bf16[1,3584,512]{2,1,0:T(8,128)(2,1)}, u32[]{:S(2)}) copy-start(bf16[1,3584,512]{2,1,0:T(8,128)(2,1)} %param.12) | copy-start | bytes 11010052
  53.3 4.3 %copy-start.3 = (bf16[8,24,3584]{2,1,0:T(8,128)(2,1)S(1)}, bf16[8,24,3584]{2,1,0:T(8,128)(2,1)}, u32[]{:S(2)}) copy-start(bf16[8,24,3584]{2,1,0:T(8,128)(2,1)} %all-gather.3.cloned.1.call-done) | copy-start | bytes 4128772
  65.7 4.0 %copy-start.4 = (bf16[1,512,3584]{2,1,0:T(8,128)(2,1)S(1)}, bf16[1,512,3584]{2,1,0:T(8,128)(2,1)}, u32[]{:S(2)}) copy-start(bf16[1,512,3584]{2,1,0:T(8,128)(2,1)} %param.13) | copy-start | bytes 11010052
  86.7 62.4 %reduce-scatter.9.cloned.1.call-start = ((), (), s32[]{:S(2)}) async-start(), calls=%async_computation.9 | async-start | bytes 2293760
  86.9 3.5 %copy-start.2 = (bf16[1,3584,512]{2,1,0:T(8,128)(2,1)S(1)}, bf16[1,3584,512]{2,1,0:T(8,128)(2,1)}, u32[]{:S(2)}) copy-start(bf16[1,3584,512]{2,1,0:T(8,128)(2,1)} %param.12) | copy-start | bytes 11010052
  126.9 32.6 %collective-permute-start = (bf16[1,24,896]{2,1,0:T(8,128)(2,1)}, bf16[1,24,896]{2,1,0:T(8,128)(2,1)}, u32[]{:S(2)}, u32[]{:S(2)}) collective-permute-start(bf16[1,24,896]{2,1,0:T(8,128)(2,1)} %copy.19), channel_id=1, source_target_pairs={{0,1},{1,0},{2,3},{3,2},{4,5},{5,4},{6,7},{7,6},{8,9},{9,8},{10,11... | collective-permute-start | bytes 129032 | tf_op jit(solution)/shard_map/ppermute | solution.py:18
  130.2 34.0 %collective-permute-start.1 = (bf16[1,24,896]{2,1,0:T(8,128)(2,1)}, bf16[1,24,896]{2,1,0:T(8,128)(2,1)}, u32[]{:S(2)}, u32[]{:S(2)}) collective-permute-start(bf16[1,24,896]{2,1,0:T(8,128)(2,1)} %copy.20), channel_id=1, source_target_pairs={{0,2},{1,3},{2,0},{3,1},{4,6},{5,7},{6,4},{7,5},{8,10},{9,11},{10,... | collective-permute-start | bytes 129032 | tf_op jit(solution)/shard_map/ppermute | solution.py:18
  133.4 33.1 %collective-permute-start.2 = (bf16[1,24,896]{2,1,0:T(8,128)(2,1)}, bf16[1,24,896]{2,1,0:T(8,128)(2,1)}, u32[]{:S(2)}, u32[]{:S(2)}) collective-permute-start(bf16[1,24,896]{2,1,0:T(8,128)(2,1)} %copy.21), channel_id=1, source_target_pairs={{0,3},{1,2},{2,1},{3,0},{4,7},{5,6},{6,5},{7,4},{8,11},{9,10},{10,... | collective-permute-start | bytes 129032 | tf_op jit(solution)/shard_map/ppermute | solution.py:18
  135.7 31.6 %collective-permute-start.3 = (bf16[1,24,896]{2,1,0:T(8,128)(2,1)}, bf16[1,24,896]{2,1,0:T(8,128)(2,1)S(1)}, u32[]{:S(2)}, u32[]{:S(2)}) collective-permute-start(bf16[1,24,896]{2,1,0:T(8,128)(2,1)} %copy.22), channel_id=1, source_target_pairs={{0,4},{1,5},{2,6},{3,7},{4,0},{5,1},{6,2},{7,3},{8,12},{9,13},{10,... | collective-permute-start | bytes 129032 | tf_op jit(solution)/shard_map/ppermute | solution.py:18
  139.3 28.1 %collective-permute-start.4 = (bf16[1,24,896]{2,1,0:T(8,128)(2,1)}, bf16[1,24,896]{2,1,0:T(8,128)(2,1)S(1)}, u32[]{:S(2)}, u32[]{:S(2)}) collective-permute-start(bf16[1,24,896]{2,1,0:T(8,128)(2,1)} %copy.23), channel_id=1, source_target_pairs={{0,5},{1,4},{2,7},{3,6},{4,1},{5,0},{6,3},{7,2},{8,13},{9,12},{10,... | collective-permute-start | bytes 129032 | tf_op jit(solution)/shard_map/ppermute | solution.py:18
  141.9 30.1 %copy-start.5 = (bf16[128,896]{1,0:T(8,128)(2,1)S(1)}, bf16[128,896]{1,0:T(8,128)(2,1)}, u32[]{:S(2)}) copy-start(bf16[128,896]{1,0:T(8,128)(2,1)} %param.8) | copy-start | bytes 688132
  154.0 25.5 %all-to-all-start.3 = ((bf16[8,24,896]{2,1,0:T(8,128)(2,1)}), bf16[8,24,896]{2,1,0:T(8,128)(2,1)S(1)}, u32[]{:S(2)}, u32[]{:S(2)}) async-start(bf16[8,24,896]{2,1,0:T(8,128)(2,1)} %copy.17), calls=%async_computation.3 | async-start | bytes 688128 | tf_op jit(solution)/shard_map/all_to_all | solution.py:109
  159.5 11.1 %collective-permute-start.5 = (bf16[1,24,896]{2,1,0:T(8,128)(2,1)S(1)}, bf16[1,24,896]{2,1,0:T(8,128)(2,1)S(1)}, u32[]{:S(2)}, u32[]{:S(2)}) collective-permute-start(bf16[1,24,896]{2,1,0:T(8,128)(2,1)S(1)} %copy.24), channel_id=1, source_target_pairs={{0,6},{1,7},{2,4},{3,5},{4,2},{5,3},{6,0},{7,1},{8,14},{9,15},{10,... | collective-permute-start | bytes 129032 | tf_op jit(solution)/shard_map/ppermute | solution.py:18
  164.2 7.7 %collective-permute-start.6 = (bf16[1,24,896]{2,1,0:T(8,128)(2,1)S(1)}, bf16[1,24,896]{2,1,0:T(8,128)(2,1)S(1)}, u32[]{:S(2)}, u32[]{:S(2)}) collective-permute-start(bf16[1,24,896]{2,1,0:T(8,128)(2,1)S(1)} %copy.25), channel_id=1, source_target_pairs={{0,7},{1,6},{2,5},{3,4},{4,3},{5,2},{6,1},{7,0},{8,15},{9,14},{10,... | collective-permute-start | bytes 129032 | tf_op jit(solution)/shard_map/ppermute | solution.py:18
Sparse Core Ops, SparseCore 0:
  28.5 17.0 all-gather.2
  47.1 18.5 all-gather.4
  86.8 29.7 reduce-scatter.6
  119.2 29.8 reduce-scatter.8
